TPU v7x, 32 devices: a whole 2x2x4 slice. The times are simulated.
32 devices in a mesh: strip: 8 (over z, x), chan: 4 (over y, core).
Axes of the slice: x: 2, y: 2, z: 4, core: 2. Of those that a mesh axis runs over, the one named last changes fastest.
Arguments:
- features: bfloat16 [512, 32, 128], P('chan', 'strip'), may hold values from -6 to 6
- first_filters: bfloat16 [512, 3, 3, 512], P('chan'), may hold values from -0.09375 to 0.09375
- second_filters: bfloat16 [512, 3, 3, 512], P('chan'), may hold values from -0.09375 to 0.09375
- out_grad: bfloat16 [512, 32, 128], P('chan', 'strip'), may hold values from -6 to 6
Outputs:
- output: bfloat16 [512, 32, 128], P('chan', 'strip')
- input_grad: bfloat16 [512, 32, 128], P('chan', 'strip')
- first_grad: float32 [512, 3, 3, 512], P('chan')
- second_grad: float32 [512, 3, 3, 512], P('chan')
All inputs are finite; a program needn't handle non-finite values.
Results may differ from a plain program's by a relative error of at most 0.005.
Values may be sent and summed in bfloat16 or wider, within the bound.
No kernel may reach another device: no remote copies, remote signals or barrier semaphores. Data moves between devices by JAX's collectives and lax.ppermute only.
A program may use at most 128 MiB of HBM per device.

v0:
```python
import jax
import jax.numpy as jnp
from jax import lax
from jax.sharding import PartitionSpec as P


def extended(cells, sides, width):
    for axis, dim in sides:
        count = lax.axis_size(axis)
        ends = count - 1
        head = lax.slice_in_dim(cells, 0, width, axis=dim)
        tail = lax.slice_in_dim(cells, cells.shape[dim] - width, cells.shape[dim], axis=dim)
        cells = jnp.concatenate(
            [
                lax.ppermute(tail, axis, [(i, (i + 1) % count) for i in range(ends)]),
                cells,
                lax.ppermute(head, axis, [((i + 1) % count, i) for i in range(ends)]),
            ],
            axis=dim,
        )
    return cells


def take_cols(field, shift):
    if shift == 0:
        return field
    edge = jnp.zeros(field.shape[:-1] + (1,), field.dtype)
    if shift > 0:
        return jnp.concatenate([field[..., 1:], edge], axis=-1)
    return jnp.concatenate([edge, field[..., :-1]], axis=-1)


def conv_fwd(padded, weight):
    chans, rows_pad, cols = padded.shape
    rows = rows_pad - 2
    outs = weight.shape[0]
    flat_w = weight.reshape(outs * 9, chans)
    taps = jnp.dot(
        flat_w, padded.reshape(chans, rows_pad * cols), preferred_element_type=jnp.float32
    )
    taps = taps.reshape(outs, 3, 3, rows_pad, cols)
    total = jnp.zeros((outs, rows, cols), jnp.float32)
    for kh in range(3):
        for kw in range(3):
            total = total + take_cols(taps[:, kh, kw, kh : kh + rows, :], kw - 1)
    return total


def back_stack(padded):
    outs, rows_pad, cols = padded.shape
    rows = rows_pad - 2
    pieces = []
    for kh in range(3):
        for kw in range(3):
            pieces.append(take_cols(padded[:, 2 - kh : 2 - kh + rows, :], 1 - kw))
    return jnp.stack(pieces, axis=1).reshape(outs * 9, rows * cols)


def conv_back_stacked(stacked, weight, rows, cols):
    outs = weight.shape[0]
    inner = weight.shape[3]
    flat_w = weight.reshape(outs * 9, inner)
    result = lax.dot_general(
        flat_w, stacked, (((0,), (0,)), ((), ())), preferred_element_type=jnp.float32
    )
    return result.reshape(inner, rows, cols)


def filter_grad(grad_out, padded):
    outs, rows, cols = grad_out.shape
    chans, rows_pad, _ = padded.shape
    pieces = []
    for kh in range(3):
        for kw in range(3):
            moved = take_cols(grad_out, 1 - kw)
            pieces.append(jnp.pad(moved, ((0, 0), (kh, 2 - kh), (0, 0))))
    stacked = jnp.stack(pieces, axis=1).reshape(outs * 9, rows_pad * cols)
    result = lax.dot_general(
        stacked,
        padded.reshape(chans, rows_pad * cols),
        (((1,), (1,)), ((), ())),
        preferred_element_type=jnp.float32,
    )
    return result.reshape(outs, 3, 3, chans)


def chan_sum_scatter(part, axis):
    count = lax.axis_size(axis)
    me = lax.axis_index(axis)
    blocks = part.reshape((count, part.shape[0] // count) + part.shape[1:])
    bit = 1
    while bit < count:
        pairs = blocks.reshape((blocks.shape[0] // 2, 2) + blocks.shape[1:])
        side = me // bit % 2
        keep = lax.dynamic_index_in_dim(pairs, side, axis=1, keepdims=False)
        send = lax.dynamic_index_in_dim(pairs, 1 - side, axis=1, keepdims=False)
        blocks = keep + lax.ppermute(send, axis, [(i, i ^ bit) for i in range(count)])
        bit *= 2
    return blocks.reshape(blocks.shape[1:])


def body(features, first_filters, second_filters, out_grad):
    blocks, rows, cols = features.shape
    dy_pad = extended(out_grad, (("strip", 1),), 1)
    dy_stack = back_stack(dy_pad)
    hidden_grad = chan_sum_scatter(conv_back_stacked(dy_stack, second_filters, rows, cols), "chan")
    x_pad = extended(features, (("strip", 1),), 1)
    x_all = lax.all_gather(x_pad, "chan", axis=0, tiled=True)
    pre_full = conv_fwd(x_all, first_filters)
    pre = pre_full.astype(jnp.bfloat16)
    hidden = jax.nn.silu(pre_full).astype(jnp.bfloat16)
    h_pad = extended(hidden, (("strip", 1),), 1)
    h_all = lax.all_gather(h_pad, "chan", axis=0, tiled=True)
    second_grad = lax.psum(filter_grad(out_grad, h_all), "strip")
    output = (features.astype(jnp.float32) + conv_fwd(h_all, second_filters)).astype(jnp.bfloat16)
    pre_val = pre.astype(jnp.float32)
    sig = jax.nn.sigmoid(pre_val)
    pre_grad = (hidden_grad * sig * (1.0 + pre_val * (1.0 - sig))).astype(jnp.bfloat16)
    da_pad = extended(pre_grad, (("strip", 1),), 1)
    second_grad, late_grad = lax.optimization_barrier((second_grad, pre_grad))
    first_grad = lax.psum(filter_grad(late_grad, x_all), "strip")
    da_stack = back_stack(da_pad)
    input_term = chan_sum_scatter(conv_back_stacked(da_stack, first_filters, rows, cols), "chan")
    input_grad = (out_grad.astype(jnp.float32) + input_term).astype(jnp.bfloat16)
    return (output, input_grad, first_grad, second_grad)


def solution(mesh):
    in_specs = (
        P("chan", "strip", None),
        P("chan", None, None, None),
        P("chan", None, None, None),
        P("chan", "strip", None),
    )
    out_specs = (
        P("chan", "strip", None),
        P("chan", "strip", None),
        P("chan", None, None, None),
        P("chan", None, None, None),
    )
    return jax.shard_map(body, mesh=mesh, in_specs=in_specs, out_specs=out_specs, check_vma=False)
```

profile of v0, /device:TPU:0, one launch (start us, length us, event | category | flops | bytes accessed | tf_op | source)
XLA Modules:
  0.0 348.0 jit_solution(8642496405318678284)
XLA Ops:
  7.2 1.0 copy.104
  8.3 4.8 %collective-permute-start.5 = (bf16[128,1,128]{0,2,1:T(8,128)(2,1)S(1)}, bf16[128,1,128]{0,2,1:T(8,128)(2,1)S(1)}, u32[]{:S(2)}, u32[]{:S(2)}) collective-permute-start(bf16[128,1,128]{0,2,1:T(8,128)(2,1)S(1)} %get-tuple-element.42), channel_id=1, source_target_pairs={{0,4},{4,8},{8,12},{12,16},{16,20},{20,24},{24,28},{1,5},{5,9},{9,... | collective-permute-start | bytes 98312 | tf_op jit(solution)/shard_map/ppermute | solution.py:15
  13.1 1.3 collective-permute-start.4
  14.4 1.0 copy.77
  16.1 1.3 collective-permute-start.1
  17.4 5.2 %collective-permute-start = (bf16[128,1,128]{0,2,1:T(8,128)(2,1)}, bf16[128,1,128]{0,2,1:T(8,128)(2,1)S(1)}, u32[]{:S(2)}, u32[]{:S(2)}) collective-permute-start(bf16[128,1,128]{0,2,1:T(8,128)(2,1)} %get-tuple-element.36), channel_id=1, source_target_pairs={{0,4},{4,8},{8,12},{12,16},{16,20},{20,24},{24,28},{1,5},{5,9},{9,... | collective-permute-start | bytes 98312 | tf_op jit(solution)/shard_map/ppermute | solution.py:15
  22.6 2.3 copy.93
  24.9 1.1 reshape.64
  26.0 2.7 copy.80
  28.7 2.2 reshape.61
  31.3 2.0 copy.110
  33.3 3.1 convolution_bitcast_fusion.3
  36.4 1.9 reshape_reshape_reshape.6
  39.3 1.4 copy.112
  40.7 8.9 %all_gather.6 = bf16[512,6,128]{0,2,1:T(8,128)(2,1)S(1)} all-gather(bf16[128,6,128]{0,2,1:T(8,128)(2,1)S(1)} %pad_maximum_fusion.1), channel_id=1, replica_groups=mesh['strip'=8,'chan'=4] {'chan'}, dimensions={0}, use_global_device_ids=true | all-gather | bytes 983040 | tf_op jit(solution)/shard_map/all_gather | solution.py:108
  51.0 3.1 convolution_bitcast_fusion.1
  55.5 5.2 %copy.81 = f32[1152,768]{1,0:T(8,128)} copy(f32[1152,768]{0,1:T(8,128)} %convolution_bitcast_fusion.1) | data formatting | bytes 7077888 | tf_op jit(solution)/shard_map/dot_general | solution.py:38
  60.7 4.8 %reshape.62 = f32[128,3,3,6,128]{4,3,2,1,0:T(8,128)} reshape(f32[1152,768]{1,0:T(8,128)} %copy.81) | data formatting | bytes 7077888 | tf_op jit(solution)/shard_map/reshape | solution.py:41
  66.9 2.3 slice_bitcast_fusion.17
  69.2 1.2 bitcast_add_fusion.1
  70.4 1.6 collective-permute-start.7
  74.7 4.3 %collective-permute-done.7 = f32[1,128,4,128]{3,2,1,0:T(4,128)S(1)} collective-permute-done((f32[1,128,4,128]{3,2,1,0:T(4,128)S(1)}, f32[1,128,4,128]{3,2,1,0:T(4,128)S(1)}, u32[]{:S(2)}, u32[]{:S(2)}) %collective-permute-start.7) | collective-permute-done | bytes 262176 | tf_op jit(solution)/shard_map/ppermute | solution.py:97
  79.0 2.0 fusion.9
  81.3 1.3 collective-permute-start.3
  82.6 5.5 %collective-permute-start.2 = (bf16[128,1,128]{2,1,0:T(2,128)(2,1)S(1)}, bf16[128,1,128]{2,1,0:T(2,128)(2,1)S(1)}, u32[]{:S(2)}, u32[]{:S(2)}) collective-permute-start(bf16[128,1,128]{2,1,0:T(2,128)(2,1)S(1)} %get-tuple-element.34), channel_id=1, source_target_pairs={{0,4},{4,8},{8,12},{12,16},{16,20},{20,24},{24,28},{1,5},{5,9},{9,... | collective-permute-start | bytes 98312 | tf_op jit(solution)/shard_map/ppermute | solution.py:15
  88.7 1.2 collective-permute-done.2
  90.2 8.8 %all_gather.7 = bf16[512,6,128]{2,0,1:T(8,128)(2,1)S(1)} all-gather(bf16[128,6,128]{2,0,1:T(8,128)(2,1)S(1)} %copy.91), channel_id=1, replica_groups=mesh['strip'=8,'chan'=4] {'chan'}, dimensions={0}, use_global_device_ids=true | all-gather | bytes 983040 | tf_op jit(solution)/shard_map/all_gather | solution.py:113
  99.3 4.3 %fusion.72 = f32[128,3,3,512]{3,0,2,1:T(8,128)} fusion(bf16[128,3,3,768]{0,3,2,1:T(8,128)(2,1)} %bitcast.57, bf16[512,768,1,1]{0,1,3,2:T(8,128)(2,1)S(1)} %bitcast.264), kind=kOutput, calls=%fused_computation.154 | convolution fusion | flops 905969664 | bytes 4915200 | tf_op jit(solution)/shard_map/dot_general | solution.py:78
  103.8 4.8 %collective-permute-start.9 = (bf16[128,1,128]{2,1,0:T(2,128)(2,1)S(1)}, bf16[128,1,128]{2,1,0:T(2,128)(2,1)S(1)}, u32[]{:S(2)}, u32[]{:S(2)}) collective-permute-start(bf16[128,1,128]{2,1,0:T(2,128)(2,1)S(1)} %get-tuple-element.32), channel_id=1, source_target_pairs={{0,4},{4,8},{8,12},{12,16},{16,20},{20,24},{24,28},{1,5},{5,9},{9,... | collective-permute-start | bytes 98312 | tf_op jit(solution)/shard_map/ppermute | solution.py:15
  108.6 1.3 collective-permute-start.8
  110.5 7.2 %collective-permute-done.8 = bf16[128,1,128]{2,1,0:T(2,128)(2,1)S(1)} collective-permute-done((bf16[128,1,128]{2,1,0:T(2,128)(2,1)S(1)}, bf16[128,1,128]{2,1,0:T(2,128)(2,1)S(1)}, u32[]{:S(2)}, u32[]{:S(2)}) %collective-permute-start.8) | collective-permute-done | bytes 32800 | tf_op jit(solution)/shard_map/ppermute | solution.py:17
  119.2 96.3 %all-reduce.47.cloned.1.call-done = f32[128,3,3,512]{3,0,2,1:T(8,128)} async-done(((f32[128,3,3,512]{3,0,2,1:T(8,128)}), f32[128,3,3,512]{3,0,2,1:T(8,128)}) %all-reduce.47.cloned.1.call-update) | async-done | bytes 2359312 | tf_op jit(solution)/shard_map/psum | solution.py:114
  222.9 3.1 copy.121
  226.0 2.5 fusion.73
  228.5 1.2 copy-done.7
  232.7 1.7 constant_dynamic-slice_fusion.2
  234.5 1.4 copy.115
  235.8 2.7 convolution_bitcast_fusion
  238.6 3.0 copy.94
  241.6 4.9 %reshape.65 = f32[128,3,3,6,128]{4,3,2,1,0:T(8,128)} reshape(f32[1152,768]{1,0:T(8,128)} %copy.94) | data formatting | bytes 7077888 | tf_op jit(solution)/shard_map/reshape | solution.py:41
  247.2 1.2 bitcast_add_fusion
  248.4 1.5 collective-permute-start.11
  250.0 2.3 slice_bitcast_fusion.8
  253.1 2.6 fusion.21
  255.7 1.5 collective-permute-done.11
  258.0 78.5 %all-reduce.49.cloned.1.call-done = f32[128,3,3,512]{3,0,2,1:T(8,128)} async-done(((f32[128,3,3,512]{3,0,2,1:T(8,128)}), f32[128,3,3,512]{3,0,2,1:T(8,128)}) %all-reduce.49.cloned.1.call-update) | async-done | bytes 2359312 | tf_op jit(solution)/shard_map/psum | solution.py:121
  336.5 3.3 copy.190
  339.7 1.4 copy.191
  (100 shorter events, 25.5 us)
Async XLA Ops:
  7.2 208.3 %all-reduce.47.cloned.1.call-start = ((), (), s32[]{:S(2)}) async-start(), calls=%async_computation | async-start | bytes 4718592 | tf_op jit(solution)/shard_map/psum | solution.py:114
  8.3 22.6 %collective-permute-start.5 = (bf16[128,1,128]{0,2,1:T(8,128)(2,1)S(1)}, bf16[128,1,128]{0,2,1:T(8,128)(2,1)S(1)}, u32[]{:S(2)}, u32[]{:S(2)}) collective-permute-start(bf16[128,1,128]{0,2,1:T(8,128)(2,1)S(1)} %get-tuple-element.42), channel_id=1, source_target_pairs={{0,4},{4,8},{8,12},{12,16},{16,20},{20,24},{24,28},{1,5},{5,9},{9,... | collective-permute-start | bytes 98312 | tf_op jit(solution)/shard_map/ppermute | solution.py:15
  13.1 17.8 %collective-permute-start.4 = (bf16[128,1,128]{0,2,1:T(8,128)(2,1)S(1)}, bf16[128,1,128]{0,2,1:T(8,128)(2,1)S(1)}, u32[]{:S(2)}, u32[]{:S(2)}) collective-permute-start(bf16[128,1,128]{0,2,1:T(8,128)(2,1)S(1)} %get-tuple-element.43), channel_id=1, source_target_pairs={{4,0},{8,4},{12,8},{16,12},{20,16},{24,20},{28,24},{5,1},{9,5},{13... | collective-permute-start | bytes 98312 | tf_op jit(solution)/shard_map/ppermute | solution.py:17
  16.1 24.6 %collective-permute-start.1 = (bf16[128,1,128]{0,2,1:T(8,128)(2,1)}, bf16[128,1,128]{0,2,1:T(8,128)(2,1)S(1)}, u32[]{:S(2)}, u32[]{:S(2)}) collective-permute-start(bf16[128,1,128]{0,2,1:T(8,128)(2,1)} %get-tuple-element.37), channel_id=1, source_target_pairs={{4,0},{8,4},{12,8},{16,12},{20,16},{24,20},{28,24},{5,1},{9,5},{13... | collective-permute-start | bytes 98312 | tf_op jit(solution)/shard_map/ppermute | solution.py:17
  17.4 23.3 %collective-permute-start = (bf16[128,1,128]{0,2,1:T(8,128)(2,1)}, bf16[128,1,128]{0,2,1:T(8,128)(2,1)S(1)}, u32[]{:S(2)}, u32[]{:S(2)}) collective-permute-start(bf16[128,1,128]{0,2,1:T(8,128)(2,1)} %get-tuple-element.36), channel_id=1, source_target_pairs={{0,4},{4,8},{8,12},{12,16},{16,20},{20,24},{24,28},{1,5},{5,9},{9,... | collective-permute-start | bytes 98312 | tf_op jit(solution)/shard_map/ppermute | solution.py:15
  25.9 7.3 %copy-start.1 = (bf16[1152,512]{1,0:T(8,128)(2,1)}, bf16[1152,512]{1,0:T(8,128)(2,1)S(1)}, u32[]{:S(2)}) copy-start(bf16[1152,512]{1,0:T(8,128)(2,1)S(1)} %reshape.64) | copy-start | bytes 3538948
  39.3 11.7 %copy-start.2 = (bf16[1152,512]{1,0:T(8,128)(2,1)S(1)}, bf16[1152,512]{1,0:T(8,128)(2,1)}, u32[]{:S(2)}) copy-start(bf16[1152,512]{1,0:T(8,128)(2,1)} %reshape.61) | copy-start | bytes 3538948
  40.7 28.5 %collective-permute-start.6 = (f32[2,128,4,128]{3,2,1,0:T(4,128)}, f32[2,128,4,128]{3,2,1,0:T(4,128)}, u32[]{:S(2)}, u32[]{:S(2)}) collective-permute-start(f32[2,128,4,128]{3,2,1,0:T(4,128)} %bitcast.33), channel_id=1, source_target_pairs={{0,1},{1,0},{2,3},{3,2},{4,5},{5,4},{6,7},{7,6},{8,9},{9,8},{10,11... | collective-permute-start | bytes 1572872 | tf_op jit(solution)/shard_map/ppermute | solution.py:97
  70.4 8.6 %collective-permute-start.7 = (f32[1,128,4,128]{3,2,1,0:T(4,128)S(1)}, f32[1,128,4,128]{3,2,1,0:T(4,128)S(1)}, u32[]{:S(2)}, u32[]{:S(2)}) collective-permute-start(f32[1,128,4,128]{3,2,1,0:T(4,128)S(1)} %constant_dynamic-slice_fusion.3), channel_id=1, source_target_pairs={{0,2},{1,3},{2,0},{3,1},{4,6},{5,7},{6,4},{7,5},{8,10},{9,11},{10,... | collective-permute-start | bytes 786440 | tf_op jit(solution)/shard_map/ppermute | solution.py:97
  81.3 7.5 %collective-permute-start.3 = (bf16[128,1,128]{2,1,0:T(2,128)(2,1)S(1)}, bf16[128,1,128]{2,1,0:T(2,128)(2,1)S(1)}, u32[]{:S(2)}, u32[]{:S(2)}) collective-permute-start(bf16[128,1,128]{2,1,0:T(2,128)(2,1)S(1)} %get-tuple-element.35), channel_id=1, source_target_pairs={{4,0},{8,4},{12,8},{16,12},{20,16},{24,20},{28,24},{5,1},{9,5},{13... | collective-permute-start | bytes 98312 | tf_op jit(solution)/shard_map/ppermute | solution.py:17
  82.6 7.4 %collective-permute-start.2 = (bf16[128,1,128]{2,1,0:T(2,128)(2,1)S(1)}, bf16[128,1,128]{2,1,0:T(2,128)(2,1)S(1)}, u32[]{:S(2)}, u32[]{:S(2)}) collective-permute-start(bf16[128,1,128]{2,1,0:T(2,128)(2,1)S(1)} %get-tuple-element.34), channel_id=1, source_target_pairs={{0,4},{4,8},{8,12},{12,16},{16,20},{20,24},{24,28},{1,5},{5,9},{9,... | collective-permute-start | bytes 98312 | tf_op jit(solution)/shard_map/ppermute | solution.py:15
  99.3 4.3 %copy-start = (bf16[512,6,128]{0,2,1:T(8,128)(2,1)}, bf16[512,6,128]{0,2,1:T(8,128)(2,1)S(1)}, u32[]{:S(2)}) copy-start(bf16[512,6,128]{0,2,1:T(8,128)(2,1)S(1)} %copy.92) | copy-start | bytes 2359300
  103.6 232.9 %all-reduce.49.cloned.1.call-start = ((), (), s32[]{:S(2)}) async-start(), calls=%async_computation.1 | async-start | bytes 4718592 | tf_op jit(solution)/shard_map/psum | solution.py:121
  103.8 6.7 %collective-permute-start.9 = (bf16[128,1,128]{2,1,0:T(2,128)(2,1)S(1)}, bf16[128,1,128]{2,1,0:T(2,128)(2,1)S(1)}, u32[]{:S(2)}, u32[]{:S(2)}) collective-permute-start(bf16[128,1,128]{2,1,0:T(2,128)(2,1)S(1)} %get-tuple-element.32), channel_id=1, source_target_pairs={{0,4},{4,8},{8,12},{12,16},{16,20},{20,24},{24,28},{1,5},{5,9},{9,... | collective-permute-start | bytes 98312 | tf_op jit(solution)/shard_map/ppermute | solution.py:15
  108.6 9.0 %collective-permute-start.8 = (bf16[128,1,128]{2,1,0:T(2,128)(2,1)S(1)}, bf16[128,1,128]{2,1,0:T(2,128)(2,1)S(1)}, u32[]{:S(2)}, u32[]{:S(2)}) collective-permute-start(bf16[128,1,128]{2,1,0:T(2,128)(2,1)S(1)} %get-tuple-element.33), channel_id=1, source_target_pairs={{4,0},{8,4},{12,8},{16,12},{20,16},{24,20},{28,24},{5,1},{9,5},{13... | collective-permute-start | bytes 98312 | tf_op jit(solution)/shard_map/ppermute | solution.py:17
  119.2 96.4 %copy-start.6 = (bf16[128,9,4,128]{3,2,0,1:T(4,128)(2,1)}, bf16[128,9,4,128]{3,2,0,1:T(4,128)(2,1)S(1)}, u32[]{:S(2)}) copy-start(bf16[128,9,4,128]{3,2,0,1:T(4,128)(2,1)S(1)} %bitcast_dynamic-update-slice_fusion.19) | copy-start | bytes 3538948
  228.5 1.3 copy-start.7
  229.9 1.3 copy-start.3
  235.8 11.4 %collective-permute-start.10 = (f32[2,128,4,128]{3,2,1,0:T(4,128)}, f32[2,128,4,128]{3,2,1,0:T(4,128)}, u32[]{:S(2)}, u32[]{:S(2)}) collective-permute-start(f32[2,128,4,128]{3,2,1,0:T(4,128)} %bitcast.46), channel_id=1, source_target_pairs={{0,1},{1,0},{2,3},{3,2},{4,5},{5,4},{6,7},{7,6},{8,9},{9,8},{10,11... | collective-permute-start | bytes 1572872 | tf_op jit(solution)/shard_map/ppermute | solution.py:97
  241.6 4.9 %copy-start.5 = (f32[2,1,128,4,128]{2,1,0,4,3:T(1,128)S(1)}, f32[2,1,128,4,128]{2,1,0,4,3:T(1,128)}, u32[]{:S(2)}) copy-start(f32[2,1,128,4,128]{2,1,0,4,3:T(1,128)} %get-tuple-element.22) | copy-start | bytes 1572868
  248.4 8.8 %collective-permute-start.11 = (f32[1,128,4,128]{3,2,1,0:T(4,128)S(1)}, f32[1,128,4,128]{3,2,1,0:T(4,128)S(1)}, u32[]{:S(2)}, u32[]{:S(2)}) collective-permute-start(f32[1,128,4,128]{3,2,1,0:T(4,128)S(1)} %constant_dynamic-slice_fusion), channel_id=1, source_target_pairs={{0,2},{1,3},{2,0},{3,1},{4,6},{5,7},{6,4},{7,5},{8,10},{9,11},{10,... | collective-permute-start | bytes 786440 | tf_op jit(solution)/shard_map/ppermute | solution.py:97
  252.2 0.9 copy-start.8
  252.7 4.5 %copy-start.9 = (bf16[128,4,128]{2,1,0:T(4,128)(2,1)S(1)}, bf16[128,4,128]{2,1,0:T(4,128)(2,1)}, u32[]{:S(2)}) copy-start(bf16[128,4,128]{2,1,0:T(4,128)(2,1)} %param.7) | copy-start | bytes 393220
  258.0 81.8 %copy-start.4 = (f32[128,3,3,512]{3,0,2,1:T(8,128)S(1)}, f32[128,3,3,512]{3,0,2,1:T(8,128)}, u32[]{:S(2)}) copy-start(f32[128,3,3,512]{3,0,2,1:T(8,128)} %all-reduce.47.cloned.1.call-done) | copy-start | bytes 7077892
Sparse Core Ops, SparseCore 0:
  103.7 111.7 all-reduce.46
  228.7 107.7 all-reduce.48
where the time goes:
time: 349 us; the launch traced here: 348 us
  waiting for transfers between devices  190 us (54%)
  local copies, waits for them, and re-layouts  70.9 us (20%)
  starting transfers between devices  28.7 us (8%)
  blocking collectives  17.7 us (5%)
  matrix products  16.6 us (5%)
  between operations  14.5 us (4%)
  other arithmetic  10 us (3%)
    psum x1, waiting for transfers between devices, body(): second_grad = lax.psum(filter_grad(out_grad, h_all), 'strip')  96.3 us
    psum x1, waiting for transfers between devices, body(): first_grad = lax.psum(filter_grad(late_grad, x_all), 'strip')  78.5 us
    unnamed x52, local copies, waits for them, and re-layouts  26.1 us
    ppermute x4, starting transfers between devices, extended(): lax.ppermute(tail, axis, [(i, (i + 1) % count) for i in range(ends)])  20.3 us
    reshape x2, local copies, waits for them, and re-layouts, conv_fwd(): taps = taps.reshape(outs, 3, 3, rows_pad, cols)  9.65 us
    all_gather x1, blocking collectives, body(): x_all = lax.all_gather(x_pad, 'chan', axis=0, tiled=True)  8.87 us
    all_gather x1, blocking collectives, body(): h_all = lax.all_gather(h_pad, 'chan', axis=0, tiled=True)  8.81 us
    dot_general x2, local copies, waits for them, and re-layouts, conv_fwd(): jnp.dot(flat_w, padded.reshape(chans, rows_pad * cols), preferred_element...  8.26 us
  transfers between devices with their start and end apart: 14, of which 7 were waited for; matrix products, arithmetic and copies ran while one was open for 20% of the time, Pallas kernels for 0%

commit v1 on v0

--- a/solution.py
+++ b/solution.py
@@ -105,7 +105,14 @@
     dy_stack = back_stack(dy_pad)
     hidden_grad = chan_sum_scatter(conv_back_stacked(dy_stack, second_filters, rows, cols), "chan")
     x_pad = extended(features, (("strip", 1),), 1)
-    x_all = lax.all_gather(x_pad, "chan", axis=0, tiled=True)
+    ways, here = (lax.axis_size("chan"), lax.axis_index("chan"))
+    x_all, reach = (x_pad, 1)
+    while reach < ways:
+        theirs = lax.ppermute(x_all, "chan", [(d, d ^ reach) for d in range(ways)])
+        mine_first = jnp.concatenate([x_all, theirs], axis=0)
+        theirs_first = jnp.concatenate([theirs, x_all], axis=0)
+        x_all = jnp.where(here & reach == 0, mine_first, theirs_first)
+        reach = 2 * reach
     pre_full = conv_fwd(x_all, first_filters)
     pre = pre_full.astype(jnp.bfloat16)
     hidden = jax.nn.silu(pre_full).astype(jnp.bfloat16)

time: 349 us -> 331 us (0.948)
  local copies, waits for them, and re-layouts: 70.9 us -> 59.8 us
  blocking collectives: 17.7 us -> 8.81 us
    all_gather x1 -> x0, blocking collectives: 8.87 us -> none  [body(): x_all = lax.all_gather(x_pad, 'chan', axis=0, tiled=True)]
    ppermute x0 -> x2, waiting for transfers between devices: none -> 8.12 us  [body(): theirs = lax.ppermute(x_all, 'chan', [(d, d ^ reach) for d in range(ways)])]
    unnamed x52 -> x68, local copies, waits for them, and re-layouts: 26.1 us -> 20.2 us
    ppermute x4, waiting for transfers between devices: 5.8 us -> 1.5 us  [chan_sum_scatter(): lax.ppermute(send, axis, [(i, i ^ bit) for i in range(count)])]
    psum x1, waiting for transfers between devices: 96.3 us -> 92.6 us  [body(): second_grad = lax.psum(filter_grad(out_grad, h_all), 'strip')]
  transfers between devices with their start and end apart: 14 -> 16, of which waited for: 7 -> 8; matrix products, arithmetic and copies ran while one was open for 20% -> 20% of each run, Pallas kernels for 0% -> 0%
where the time goes in v1:
time: 331 us; the launch traced here: 330 us
  waiting for transfers between devices  189 us (57%)
  local copies, waits for them, and re-layouts  59.8 us (18%)
  starting transfers between devices  29.8 us (9%)
  matrix products  16.2 us (5%)
  between operations  14.7 us (4%)
  other arithmetic  11.9 us (4%)
  blocking collectives  8.81 us (3%)
    psum x1, waiting for transfers between devices, body(): second_grad = lax.psum(filter_grad(out_grad, h_all), 'strip')  92.6 us
    psum x1, waiting for transfers between devices, body(): first_grad = lax.psum(filter_grad(late_grad, x_all), 'strip')  76.9 us
    ppermute x4, starting transfers between devices, extended(): lax.ppermute(tail, axis, [(i, (i + 1) % count) for i in range(ends)])  20.3 us
    unnamed x68, local copies, waits for them, and re-layouts  20.2 us
    all_gather x1, blocking collectives, body(): h_all = lax.all_gather(h_pad, 'chan', axis=0, tiled=True)  8.81 us
    ppermute x2, waiting for transfers between devices, body(): theirs = lax.ppermute(x_all, 'chan', [(d, d ^ reach) for d in range(ways)])  8.12 us
    reshape x2, local copies, waits for them, and re-layouts, conv_fwd(): taps = taps.reshape(outs, 3, 3, rows_pad, cols)  7.57 us
    ppermute x4, waiting for transfers between devices, extended(): lax.ppermute(head, axis, [((i + 1) % count, i) for i in range(ends)])  7.4 us
  transfers between devices with their start and end apart: 16, of which 8 were waited for; matrix products, arithmetic and copies ran while one was open for 20% of the time, Pallas kernels for 0%

profile of v1, /device:TPU:0, one launch (start us, length us, event | category | flops | bytes accessed | tf_op | source)
XLA Modules:
  0.0 329.8 jit_solution(7052360698702688692)
XLA Ops:
  7.2 1.0 copy.104
  8.3 4.8 %collective-permute-start.7 = (bf16[128,1,128]{0,2,1:T(8,128)(2,1)S(1)}, bf16[128,1,128]{0,2,1:T(8,128)(2,1)S(1)}, u32[]{:S(2)}, u32[]{:S(2)}) collective-permute-start(bf16[128,1,128]{0,2,1:T(8,128)(2,1)S(1)} %get-tuple-element.42), channel_id=1, source_target_pairs={{0,4},{4,8},{8,12},{12,16},{16,20},{20,24},{24,28},{1,5},{5,9},{9,... | collective-permute-start | bytes 98312 | tf_op jit(solution)/shard_map/ppermute | solution.py:15
  13.1 1.3 collective-permute-start.6
  14.4 1.0 copy.77
  15.5 1.3 collective-permute-start.1
  16.8 5.2 %collective-permute-start = (bf16[128,1,128]{0,2,1:T(8,128)(2,1)S(1)}, bf16[128,1,128]{0,2,1:T(8,128)(2,1)S(1)}, u32[]{:S(2)}, u32[]{:S(2)}) collective-permute-start(bf16[128,1,128]{0,2,1:T(8,128)(2,1)S(1)} %get-tuple-element.36), channel_id=1, source_target_pairs={{0,4},{4,8},{8,12},{12,16},{16,20},{20,24},{24,28},{1,5},{5,9},{9,... | collective-permute-start | bytes 98312 | tf_op jit(solution)/shard_map/ppermute | solution.py:15
  22.0 2.3 copy.93
  24.3 1.1 reshape.69
  25.4 2.7 copy.80
  28.1 2.2 reshape.66
  30.7 2.0 copy.110
  32.7 3.1 convolution_bitcast_fusion.3
  35.8 1.9 reshape_reshape_reshape.6
  37.7 0.9 constant_dynamic-slice_fusion.5
  41.2 1.2 copy-done.3
  42.5 1.6 collective-permute-start.3
  46.4 8.1 %collective-permute-done.3 = bf16[256,6,128]{0,2,1:T(8,128)(2,1)S(1)} collective-permute-done((bf16[256,6,128]{0,2,1:T(8,128)(2,1)S(1)}, bf16[256,6,128]{0,2,1:T(8,128)(2,1)S(1)}, u32[]{:S(2)}, u32[]{:S(2)}) %collective-permute-start.3) | collective-permute-done | bytes 393248 | tf_op jit(solution)/shard_map/ppermute | solution.py:111
  55.3 3.0 convolution_bitcast_fusion.1
  58.3 3.3 copy.81
  61.6 2.7 reshape.67
  64.3 2.3 slice_bitcast_fusion.17
  67.6 2.2 fusion.11
  70.1 1.3 collective-permute-start.5
  71.4 5.5 %collective-permute-start.4 = (bf16[128,1,128]{2,1,0:T(2,128)(2,1)S(1)}, bf16[128,1,128]{2,1,0:T(2,128)(2,1)S(1)}, u32[]{:S(2)}, u32[]{:S(2)}) collective-permute-start(bf16[128,1,128]{2,1,0:T(2,128)(2,1)S(1)} %get-tuple-element.34), channel_id=1, source_target_pairs={{0,4},{4,8},{8,12},{12,16},{16,20},{20,24},{24,28},{1,5},{5,9},{9,... | collective-permute-start | bytes 98312 | tf_op jit(solution)/shard_map/ppermute | solution.py:15
  77.2 1.6 collective-permute-done.4
  79.0 8.8 %all_gather.3 = bf16[512,6,128]{2,0,1:T(8,128)(2,1)S(1)} all-gather(bf16[128,6,128]{2,0,1:T(8,128)(2,1)S(1)} %copy.91), channel_id=1, replica_groups=mesh['strip'=8,'chan'=4] {'chan'}, dimensions={0}, use_global_device_ids=true | all-gather | bytes 983040 | tf_op jit(solution)/shard_map/all_gather | solution.py:120
  88.1 2.5 fusion.76
  90.8 4.8 %collective-permute-start.11 = (bf16[128,1,128]{2,1,0:T(2,128)(2,1)S(1)}, bf16[128,1,128]{2,1,0:T(2,128)(2,1)S(1)}, u32[]{:S(2)}, u32[]{:S(2)}) collective-permute-start(bf16[128,1,128]{2,1,0:T(2,128)(2,1)S(1)} %get-tuple-element.32), channel_id=1, source_target_pairs={{0,4},{4,8},{8,12},{12,16},{16,20},{20,24},{24,28},{1,5},{5,9},{9,... | collective-permute-start | bytes 98312 | tf_op jit(solution)/shard_map/ppermute | solution.py:15
  95.7 1.3 collective-permute-start.10
  97.6 7.2 %collective-permute-done.10 = bf16[128,1,128]{2,1,0:T(2,128)(2,1)S(1)} collective-permute-done((bf16[128,1,128]{2,1,0:T(2,128)(2,1)S(1)}, bf16[128,1,128]{2,1,0:T(2,128)(2,1)S(1)}, u32[]{:S(2)}, u32[]{:S(2)}) %collective-permute-start.10) | collective-permute-done | bytes 32800 | tf_op jit(solution)/shard_map/ppermute | solution.py:17
  106.8 1.0 fusion.56
  110.0 92.6 %all-reduce.47.cloned.1.call-done = f32[128,3,3,512]{3,0,2,1:T(8,128)} async-done(((f32[128,3,3,512]{3,0,2,1:T(8,128)}), f32[128,3,3,512]{3,0,2,1:T(8,128)}) %all-reduce.47.cloned.1.call-update) | async-done | bytes 2359312 | tf_op jit(solution)/shard_map/psum | solution.py:121
  203.9 2.4 copy.121
  206.4 4.0 %fusion.4 = f32[128,3,3,512]{3,0,2,1:T(8,128)} fusion(bf16[128,3,3,768]{0,3,2,1:T(8,128)(2,1)} %bitcast.265, bf16[256,768]{0,1:T(8,128)(2,1)S(1)} %bitcast.278, bf16[256,768]{0,1:T(8,128)(2,1)S(1)} %copy-done.15, pred[]{:T(512)S(6)} %eq.11), kind=kOutput, calls=%fused_computation.9 | convolution fusion | flops 909508608 | bytes 4915201 | tf_op jit(solution)/shard_map/dot_general | solution.py:78
  212.8 1.7 copy.113
  216.1 1.7 constant_dynamic-slice_fusion.2
  217.8 1.4 copy.115
  219.2 2.7 convolution_bitcast_fusion
  221.9 3.1 copy.94
  225.0 4.9 %reshape.70 = f32[128,3,3,6,128]{4,3,2,1,0:T(8,128)} reshape(f32[1152,768]{1,0:T(8,128)} %copy.94) | data formatting | bytes 7077888 | tf_op jit(solution)/shard_map/reshape | solution.py:41
  230.6 1.2 bitcast_add_fusion
  231.8 1.6 collective-permute-start.13
  233.4 2.3 slice_bitcast_fusion.8
  236.6 2.6 fusion.23
  239.2 1.5 collective-permute-done.13
  241.4 76.9 %all-reduce.49.cloned.1.call-done = f32[128,3,3,512]{3,0,2,1:T(8,128)} async-done(((f32[128,3,3,512]{3,0,2,1:T(8,128)}), f32[128,3,3,512]{3,0,2,1:T(8,128)}) %all-reduce.49.cloned.1.call-update) | async-done | bytes 2359312 | tf_op jit(solution)/shard_map/psum | solution.py:128
  318.3 3.3 copy.190
  321.6 1.4 copy.191
  (121 shorter events, 20.9 us)
Async XLA Ops:
  7.2 195.4 %all-reduce.47.cloned.1.call-start = ((), (), s32[]{:S(2)}) async-start(), calls=%async_computation | async-start | bytes 4718592 | tf_op jit(solution)/shard_map/psum | solution.py:121
  8.3 22.0 %collective-permute-start.7 = (bf16[128,1,128]{0,2,1:T(8,128)(2,1)S(1)}, bf16[128,1,128]{0,2,1:T(8,128)(2,1)S(1)}, u32[]{:S(2)}, u32[]{:S(2)}) collective-permute-start(bf16[128,1,128]{0,2,1:T(8,128)(2,1)S(1)} %get-tuple-element.42), channel_id=1, source_target_pairs={{0,4},{4,8},{8,12},{12,16},{16,20},{20,24},{24,28},{1,5},{5,9},{9,... | collective-permute-start | bytes 98312 | tf_op jit(solution)/shard_map/ppermute | solution.py:15
  13.1 17.2 %collective-permute-start.6 = (bf16[128,1,128]{0,2,1:T(8,128)(2,1)S(1)}, bf16[128,1,128]{0,2,1:T(8,128)(2,1)S(1)}, u32[]{:S(2)}, u32[]{:S(2)}) collective-permute-start(bf16[128,1,128]{0,2,1:T(8,128)(2,1)S(1)} %get-tuple-element.43), channel_id=1, source_target_pairs={{4,0},{8,4},{12,8},{16,12},{20,16},{24,20},{28,24},{5,1},{9,5},{13... | collective-permute-start | bytes 98312 | tf_op jit(solution)/shard_map/ppermute | solution.py:17
  15.5 24.8 %collective-permute-start.1 = (bf16[128,1,128]{0,2,1:T(8,128)(2,1)S(1)}, bf16[128,1,128]{0,2,1:T(8,128)(2,1)S(1)}, u32[]{:S(2)}, u32[]{:S(2)}) collective-permute-start(bf16[128,1,128]{0,2,1:T(8,128)(2,1)S(1)} %get-tuple-element.37), channel_id=1, source_target_pairs={{4,0},{8,4},{12,8},{16,12},{20,16},{24,20},{28,24},{5,1},{9,5},{13... | collective-permute-start | bytes 98312 | tf_op jit(solution)/shard_map/ppermute | solution.py:17
  16.8 23.5 %collective-permute-start = (bf16[128,1,128]{0,2,1:T(8,128)(2,1)S(1)}, bf16[128,1,128]{0,2,1:T(8,128)(2,1)S(1)}, u32[]{:S(2)}, u32[]{:S(2)}) collective-permute-start(bf16[128,1,128]{0,2,1:T(8,128)(2,1)S(1)} %get-tuple-element.36), channel_id=1, source_target_pairs={{0,4},{4,8},{8,12},{12,16},{16,20},{20,24},{24,28},{1,5},{5,9},{9,... | collective-permute-start | bytes 98312 | tf_op jit(solution)/shard_map/ppermute | solution.py:15
  25.3 7.3 %copy-start.1 = (bf16[1152,512]{1,0:T(8,128)(2,1)}, bf16[1152,512]{1,0:T(8,128)(2,1)S(1)}, u32[]{:S(2)}) copy-start(bf16[1152,512]{1,0:T(8,128)(2,1)S(1)} %reshape.69) | copy-start | bytes 3538948
  38.7 2.3 copy-start.7
  39.4 4.8 %collective-permute-start.8 = (f32[2,128,4,128]{3,2,1,0:T(4,128)S(1)}, f32[2,128,4,128]{3,2,1,0:T(4,128)S(1)}, u32[]{:S(2)}, u32[]{:S(2)}) collective-permute-start(f32[2,128,4,128]{3,2,1,0:T(4,128)S(1)} %bitcast.276), channel_id=1, source_target_pairs={{0,1},{1,0},{2,3},{3,2},{4,5},{5,4},{6,7},{7,6},{8,9},{9,8},{10,11... | collective-permute-start | bytes 1572872 | tf_op jit(solution)/shard_map/ppermute | solution.py:97
  40.3 2.1 collective-permute-start.2
  41.2 1.2 copy-start.3
  42.5 12.8 %copy-start.10 = (bf16[1152,512]{1,0:T(8,128)(2,1)S(1)}, bf16[1152,512]{1,0:T(8,128)(2,1)}, u32[]{:S(2)}) copy-start(bf16[1152,512]{1,0:T(8,128)(2,1)} %reshape.66) | copy-start | bytes 3538948
  42.5 12.0 %collective-permute-start.3 = (bf16[256,6,128]{0,2,1:T(8,128)(2,1)S(1)}, bf16[256,6,128]{0,2,1:T(8,128)(2,1)S(1)}, u32[]{:S(2)}, u32[]{:S(2)}) collective-permute-start(bf16[256,6,128]{0,2,1:T(8,128)(2,1)S(1)} %maximum_select_fusion.2), channel_id=1, source_target_pairs={{0,2},{1,3},{2,0},{3,1},{4,6},{5,7},{6,4},{7,5},{8,10},{9,11},{10,... | collective-permute-start | bytes 1179656 | tf_op jit(solution)/shard_map/ppermute | solution.py:111
  44.2 10.3 %copy-start.14 = (bf16[256,768]{0,1:T(8,128)(2,1)}, bf16[256,768]{0,1:T(8,128)(2,1)S(1)}, u32[]{:S(2)}) copy-start(bf16[256,768]{0,1:T(8,128)(2,1)S(1)} %maximum_select_fusion.1) | copy-start | bytes 1179652
  44.4 0.8 copy-start.5
  45.9 21.3 %collective-permute-start.9 = (f32[1,128,4,128]{3,2,1,0:T(4,128)}, f32[1,128,4,128]{3,2,1,0:T(4,128)}, u32[]{:S(2)}, u32[]{:S(2)}) collective-permute-start(f32[1,128,4,128]{3,2,1,0:T(4,128)} %constant_dynamic-slice_fusion.3), channel_id=1, source_target_pairs={{0,2},{1,3},{2,0},{3,1},{4,6},{5,7},{6,4},{7,5},{8,10},{9,11},{10,... | collective-permute-start | bytes 786440 | tf_op jit(solution)/shard_map/ppermute | solution.py:97
  54.6 0.7 copy-start.16
  66.6 1.0 copy-start.6
  67.6 9.3 %copy-start.4 = (bf16[128,9,6,128]{0,3,2,1:T(8,128)(2,1)S(1)}, bf16[128,9,6,128]{0,3,2,1:T(8,128)(2,1)}, u32[]{:S(2)}) copy-start(bf16[128,9,6,128]{0,3,2,1:T(8,128)(2,1)} %copy-done.3) | copy-start | bytes 5308420
  67.6 9.3 %copy-start.8 = (bf16[128,4,128]{0,2,1:T(8,128)(2,1)S(1)}, bf16[128,4,128]{0,2,1:T(8,128)(2,1)}, u32[]{:S(2)}) copy-start(bf16[128,4,128]{0,2,1:T(8,128)(2,1)} %copy-done.7) | copy-start | bytes 393220
  70.1 7.1 %collective-permute-start.5 = (bf16[128,1,128]{2,1,0:T(2,128)(2,1)S(1)}, bf16[128,1,128]{2,1,0:T(2,128)(2,1)S(1)}, u32[]{:S(2)}, u32[]{:S(2)}) collective-permute-start(bf16[128,1,128]{2,1,0:T(2,128)(2,1)S(1)} %get-tuple-element.35), channel_id=1, source_target_pairs={{4,0},{8,4},{12,8},{16,12},{20,16},{24,20},{28,24},{5,1},{9,5},{13... | collective-permute-start | bytes 98312 | tf_op jit(solution)/shard_map/ppermute | solution.py:17
  71.4 7.3 %collective-permute-start.4 = (bf16[128,1,128]{2,1,0:T(2,128)(2,1)S(1)}, bf16[128,1,128]{2,1,0:T(2,128)(2,1)S(1)}, u32[]{:S(2)}, u32[]{:S(2)}) collective-permute-start(bf16[128,1,128]{2,1,0:T(2,128)(2,1)S(1)} %get-tuple-element.34), channel_id=1, source_target_pairs={{0,4},{4,8},{8,12},{12,16},{16,20},{20,24},{24,28},{1,5},{5,9},{9,... | collective-permute-start | bytes 98312 | tf_op jit(solution)/shard_map/ppermute | solution.py:15
  88.1 2.5 copy-start
  90.7 227.6 %all-reduce.49.cloned.1.call-start = ((), (), s32[]{:S(2)}) async-start(), calls=%async_computation.1 | async-start | bytes 4718592 | tf_op jit(solution)/shard_map/psum | solution.py:128
  90.8 6.7 %collective-permute-start.11 = (bf16[128,1,128]{2,1,0:T(2,128)(2,1)S(1)}, bf16[128,1,128]{2,1,0:T(2,128)(2,1)S(1)}, u32[]{:S(2)}, u32[]{:S(2)}) collective-permute-start(bf16[128,1,128]{2,1,0:T(2,128)(2,1)S(1)} %get-tuple-element.32), channel_id=1, source_target_pairs={{0,4},{4,8},{8,12},{12,16},{16,20},{20,24},{24,28},{1,5},{5,9},{9,... | collective-permute-start | bytes 98312 | tf_op jit(solution)/shard_map/ppermute | solution.py:15
  95.7 9.0 %collective-permute-start.10 = (bf16[128,1,128]{2,1,0:T(2,128)(2,1)S(1)}, bf16[128,1,128]{2,1,0:T(2,128)(2,1)S(1)}, u32[]{:S(2)}, u32[]{:S(2)}) collective-permute-start(bf16[128,1,128]{2,1,0:T(2,128)(2,1)S(1)} %get-tuple-element.33), channel_id=1, source_target_pairs={{4,0},{8,4},{12,8},{16,12},{20,16},{24,20},{28,24},{5,1},{9,5},{13... | collective-permute-start | bytes 98312 | tf_op jit(solution)/shard_map/ppermute | solution.py:17
  203.9 2.4 copy-start.15
  203.9 2.4 copy-start.17
  211.1 3.4 %copy-start.11 = (bf16[1152,512]{1,0:T(8,128)(2,1)S(1)}, bf16[1152,512]{1,0:T(8,128)(2,1)}, u32[]{:S(2)}) copy-start(bf16[1152,512]{1,0:T(8,128)(2,1)} %reshape.66) | copy-start | bytes 3538948
  219.2 11.4 %collective-permute-start.12 = (f32[2,128,4,128]{3,2,1,0:T(4,128)}, f32[2,128,4,128]{3,2,1,0:T(4,128)}, u32[]{:S(2)}, u32[]{:S(2)}) collective-permute-start(f32[2,128,4,128]{3,2,1,0:T(4,128)} %bitcast.48), channel_id=1, source_target_pairs={{0,1},{1,0},{2,3},{3,2},{4,5},{5,4},{6,7},{7,6},{8,9},{9,8},{10,11... | collective-permute-start | bytes 1572872 | tf_op jit(solution)/shard_map/ppermute | solution.py:97
  225.0 4.9 %copy-start.9 = (f32[2,1,128,4,128]{2,1,0,4,3:T(1,128)S(1)}, f32[2,1,128,4,128]{2,1,0,4,3:T(1,128)}, u32[]{:S(2)}) copy-start(f32[2,1,128,4,128]{2,1,0,4,3:T(1,128)} %get-tuple-element.22) | copy-start | bytes 1572868
  231.8 8.8 %collective-permute-start.13 = (f32[1,128,4,128]{3,2,1,0:T(4,128)S(1)}, f32[1,128,4,128]{3,2,1,0:T(4,128)S(1)}, u32[]{:S(2)}, u32[]{:S(2)}) collective-permute-start(f32[1,128,4,128]{3,2,1,0:T(4,128)S(1)} %constant_dynamic-slice_fusion), channel_id=1, source_target_pairs={{0,2},{1,3},{2,0},{3,1},{4,6},{5,7},{6,4},{7,5},{8,10},{9,11},{10,... | collective-permute-start | bytes 786440 | tf_op jit(solution)/shard_map/ppermute | solution.py:97
  235.7 0.9 copy-start.12
  236.1 4.5 %copy-start.13 = (bf16[128,4,128]{2,1,0:T(4,128)(2,1)S(1)}, bf16[128,4,128]{2,1,0:T(4,128)(2,1)}, u32[]{:S(2)}) copy-start(bf16[128,4,128]{2,1,0:T(4,128)(2,1)} %param.7) | copy-start | bytes 393220
  241.4 80.2 %copy-start.2 = (f32[128,3,3,512]{3,0,2,1:T(8,128)S(1)}, f32[128,3,3,512]{3,0,2,1:T(8,128)}, u32[]{:S(2)}) copy-start(f32[128,3,3,512]{3,0,2,1:T(8,128)} %all-reduce.47.cloned.1.call-done) | copy-start | bytes 7077892
Sparse Core Ops, SparseCore 0:
  90.8 111.7 all-reduce.46
  210.5 107.7 all-reduce.48
